TPU v7x, 32 devices: a whole 2x2x4 slice. The times are simulated.
32 devices in a mesh: img: 4 (over y, core), slab: 8 (over z, x).
Axes of the slice: x: 2, y: 2, z: 4, core: 2. Of those that a mesh axis runs over, the one named last changes fastest.
Arguments:
- images: bfloat16 [32, 400, 400], P(('img', 'slab')), may hold values from -1500 to 1500, as said below
- micrograph: int32 [32], P(('img', 'slab')), may hold values from 0 to 63
- defocus: float32 [64], replicated, may hold values from 30 to 90
- target_slab: int32 [32, 8, 1], P(('img', 'slab')), may hold values from 0 to 7; in each aligned block of 8 rows (0 to 7, 8 to 15, ..., all dimensions but the last counted through in order) at most 2 rows name the same one
- target_plane: int32 [32, 8], P(('img', 'slab')), may hold values from 0 to 1
- target_rows: int32 [32, 8], P(('img', 'slab')), may hold values from 0 to 7
- shift_index: int32 [32, 8], P(('img', 'slab')), may hold values from 0 to 7
- volume: bfloat16 [16, 128, 800], P('slab'), may hold values from -6 to 6
Outputs:
- residual: bfloat16 [32, 400, 400], P(('img', 'slab'))
- reconstruction: float32 [16, 128, 800], P('slab', 'img')
Inputs may be any that keep to these rules, and one draw needn't show every extreme that they name: `target_slab`: in the 8 routed blocks of one device (aligned blocks of rows, particle by particle), no slab is named more than 2 times, a bound that some block reaches. `images`: real pixel values.
All inputs are finite; a program needn't handle non-finite values.
Results may differ from a plain program's by a relative error of at most 0.013.
Values may be sent and summed in bfloat16 or wider, within the bound.
No kernel may reach another device: no remote copies, remote signals or barrier semaphores. Data moves between devices by JAX's collectives and lax.ppermute only.
A program may use at most 128 MiB of HBM per device.

v0:
```python
import math
import jax
import jax.numpy as jnp
from jax import lax
from jax.sharding import PartitionSpec as P

RB = 16
LOW = 4
WL = 8


def dft_tables(box_size):
    positions = jnp.arange(box_size, dtype=jnp.int32)
    phase_steps = positions[:, None] * positions[None, :] % box_size
    angles = phase_steps.astype(jnp.float32) * (2.0 * math.pi / box_size)
    return (jnp.cos(angles).astype(jnp.bfloat16), jnp.sin(angles).astype(jnp.bfloat16))


def forward_tables(cosine_table, sine_table):
    right_table = jnp.concatenate([cosine_table, -sine_table], axis=1)
    left_table = jnp.stack(
        [jnp.stack([cosine_table, sine_table]), jnp.stack([-sine_table, cosine_table])]
    )
    return (right_table, left_table)


def inverse_tables(cosine_table, sine_table):
    upper_half = jnp.concatenate([cosine_table, sine_table], axis=1)
    lower_half = jnp.concatenate([-sine_table, cosine_table], axis=1)
    back_table = jnp.concatenate([upper_half, lower_half], axis=0)
    final_table = jnp.stack([cosine_table, -sine_table])
    return (back_table, final_table)


def transform(image_block, right_table, left_table):
    batch_size, box_size = (image_block.shape[0], image_block.shape[1])
    rowwise = jnp.einsum(
        "nyx,xm->nym", image_block, right_table, preferred_element_type=jnp.float32
    ).astype(jnp.bfloat16)
    quarters = rowwise.reshape(batch_size, box_size, 2, box_size)
    spectrum = jnp.einsum(
        "ahky,nyhm->nkam", left_table, quarters, preferred_element_type=jnp.float32
    )
    return spectrum.reshape(batch_size, box_size, 2 * box_size)


def invert(difference, back_table, final_table):
    batch_size, box_size = (difference.shape[0], difference.shape[1])
    rowwise = jnp.einsum(
        "nyj,jk->nyk", difference, back_table, preferred_element_type=jnp.float32
    ).astype(jnp.bfloat16)
    quarters = rowwise.reshape(batch_size, box_size, 2, box_size)
    picture = (
        jnp.einsum("cxk,nkcm->nxm", final_table, quarters, preferred_element_type=jnp.float32)
        / box_size
    )
    return picture.astype(jnp.bfloat16)


def radius_sq(row_ids, box_size):
    half_size = box_size // 2
    columns = jnp.arange(box_size, dtype=jnp.int32)
    freq_rows = jnp.where(row_ids < half_size, row_ids, row_ids - box_size)
    freq_cols = jnp.where(columns < half_size, columns, columns - box_size)
    total = freq_rows[..., None] * freq_rows[..., None] + freq_cols * freq_cols
    return total.astype(jnp.float32) / float(half_size * half_size)


def contrast_curve(defocus_of, row_ids, box_size):
    radius = radius_sq(row_ids, box_size)
    return (-jnp.sin(defocus_of[:, None, None] * radius + 0.1)).astype(jnp.bfloat16)


def lookup_defocus(mic_ids, defocus):
    labels = jnp.arange(defocus.shape[0], dtype=jnp.int32)
    return jnp.sum(jnp.where(mic_ids[:, None] == labels[None, :], defocus[None, :], 0.0), axis=1)


def shift_halves(values, steps, box_size):
    split_shape = values.shape[:-1] + (2, box_size)
    return jnp.roll(values.reshape(split_shape), steps, axis=-1).reshape(values.shape)


def body(images, micrograph, defocus, target_slab, target_plane, target_rows, shift_index, volume):
    particles, box_size = (images.shape[0], images.shape[1])
    slab_count = lax.axis_size("slab")
    device_count = lax.axis_size("img") * slab_count
    low_rows = LOW * RB
    routed = particles * 2 * LOW
    cosine_table, sine_table = dft_tables(box_size)
    right_table, left_table = forward_tables(cosine_table, sine_table)
    back_table, final_table = inverse_tables(cosine_table, sine_table)
    spectrum = transform(images, right_table, left_table)
    real_part = spectrum[..., :box_size]
    imag_part = spectrum[..., box_size:]
    power_sum = jnp.sum(real_part * real_part + imag_part * imag_part, axis=0)
    power_all = lax.psum(power_sum, ("img", "slab"))
    noise_level = jnp.sqrt(power_all / (particles * device_count) + 1e-06)
    whitened = spectrum / jnp.concatenate([noise_level, noise_level], axis=1)
    row_all = jnp.arange(box_size, dtype=jnp.int32)[None, :]
    contrast = contrast_curve(lookup_defocus(micrograph, defocus), row_all, box_size)
    contrast_both = jnp.concatenate([contrast, contrast], axis=-1).astype(jnp.float32)
    weighted = (contrast_both * whitened).astype(jnp.bfloat16)
    low_blocks = jnp.concatenate(
        [weighted[:, :low_rows], weighted[:, box_size - low_rows :]], axis=1
    )
    low_blocks = low_blocks.reshape(routed, RB, 2 * box_size)
    destination = target_slab.reshape(routed)
    capacity = max(2, (2 * routed + slab_count - 1) // slab_count)
    member = (destination[:, None] == jnp.arange(slab_count, dtype=jnp.int32)[None, :]).astype(
        jnp.int32
    )
    before = jnp.cumsum(member, axis=0) - member
    slot_rank = jnp.sum(member * before, axis=1)
    seat_index = destination * capacity + slot_rank
    seat_count = slab_count * capacity
    live_flag = jnp.ones((routed,), jnp.int32)
    source_block = jnp.tile(jnp.arange(2 * LOW, dtype=jnp.int32), particles)
    block_info = jnp.stack(
        [
            live_flag,
            target_plane.reshape(routed),
            target_rows.reshape(routed),
            shift_index.reshape(routed),
            source_block,
            jnp.repeat(micrograph, 2 * LOW),
        ],
        axis=1,
    )
    send_blocks = (
        jnp.zeros((seat_count, RB, 2 * box_size), jnp.bfloat16).at[seat_index].set(low_blocks)
    )
    send_info = jnp.zeros((seat_count, 6), jnp.int32).at[seat_index].set(block_info)
    low_contrast = jnp.concatenate(
        [contrast[:, :low_rows], contrast[:, box_size - low_rows :]], axis=1
    )
    low_contrast = low_contrast.reshape(routed, RB, box_size)
    send_contrast = (
        jnp.zeros((seat_count, RB, box_size), jnp.bfloat16).at[seat_index].set(low_contrast)
    )
    got_blocks, got_contrast, got_info = (
        lax.all_to_all(send_blocks, "slab", split_axis=0, concat_axis=0, tiled=True),
        lax.all_to_all(send_contrast, "slab", split_axis=0, concat_axis=0, tiled=True),
        lax.all_to_all(send_info, "slab", split_axis=0, concat_axis=0, tiled=True),
    )
    live_mask = got_info[:, 0].astype(jnp.float32)[:, None, None]
    row_index = got_info[:, 2][:, None] * RB + jnp.arange(RB, dtype=jnp.int32)
    plane_index = jnp.broadcast_to(got_info[:, 1][:, None], row_index.shape)
    blend_weight = ((got_info[:, 3].astype(jnp.float32) + 0.5) / WL)[:, None, None]
    nearby = volume[plane_index, row_index].astype(jnp.float32)
    projected = (
        ((1.0 - blend_weight) * nearby + blend_weight * shift_halves(nearby, -1, box_size))
        * live_mask
    ).astype(jnp.bfloat16)
    returned_rows = lax.all_to_all(projected, "slab", split_axis=0, concat_axis=0, tiled=True)
    received = got_blocks.astype(jnp.float32)
    inserted = (1.0 - blend_weight) * received + blend_weight * shift_halves(received, 1, box_size)
    contrast_rows = got_contrast.astype(jnp.float32)
    squared = contrast_rows * contrast_rows
    weights = (1.0 - blend_weight) * squared + blend_weight * jnp.roll(squared, 1, axis=-1)
    numerator = jnp.zeros((volume.shape[0], volume.shape[1], 3 * box_size), jnp.float32)
    numerator = numerator.at[plane_index, row_index].add(
        jnp.concatenate([inserted, weights], axis=-1) * live_mask
    )
    volume_part = lax.psum_scatter(
        numerator.astype(jnp.bfloat16), "img", scatter_dimension=1, tiled=True
    ).astype(jnp.float32)
    weight_sum = volume_part[..., 2 * box_size :]
    reconstruction = volume_part[..., : 2 * box_size] / (
        jnp.concatenate([weight_sum, weight_sum], axis=-1) + 1.0
    )
    own_rows = returned_rows[seat_index].reshape(particles, 2 * low_rows, 2 * box_size)
    middle = jnp.zeros((particles, box_size - 2 * low_rows, 2 * box_size), jnp.bfloat16)
    full_projection = jnp.concatenate(
        [own_rows[:, :low_rows], middle, own_rows[:, low_rows:]], axis=1
    )
    difference = (whitened - contrast_both * full_projection.astype(jnp.float32)).astype(
        jnp.bfloat16
    )
    residual = invert(difference, back_table, final_table)
    return (residual, reconstruction)


def solution(mesh):
    in_specs = (
        P(("img", "slab"), None, None),
        P(("img", "slab")),
        P(),
        P(("img", "slab"), None, None),
        P(("img", "slab"), None),
        P(("img", "slab"), None),
        P(("img", "slab"), None),
        P("slab", None, None),
    )
    out_specs = (P(("img", "slab"), None, None), P("slab", "img", None))
    return jax.shard_map(body, mesh=mesh, in_specs=in_specs, out_specs=out_specs, check_vma=False)
```

profile of v0, /device:TPU:0, one launch (start us, length us, event | category | flops | bytes accessed | tf_op | source)
XLA Modules:
  0.0 247.4 jit_solution(15363540202320379219)
XLA Ops:
  7.2 3.5 %sine_convert_fusion = (bf16[1,400,400]{2,1,0:T(8,128)(2,1)S(1)}, bf16[1,400,400]{2,1,0:T(8,128)(2,1)S(1)}) fusion(), kind=kLoop, calls=%fused_computation.54 | loop fusion | flops 1760000 | bytes 640000 | tf_op jit(solution)/shard_map/convert_element_type | solution.py:16
  10.7 3.2 %fusion.52 = bf16[1,400,400]{2,1,0:T(8,128)(2,1)S(1)} fusion(), kind=kLoop, calls=%fused_computation.85 | loop fusion | flops 2080000 | bytes 320000 | tf_op jit(solution)/shard_map/neg | solution.py:20
  13.9 3.2 %cosine_convert_fusion.1 = bf16[400,400]{1,0:T(8,128)(2,1)S(1)} fusion(), kind=kLoop, calls=%fused_computation.60 | loop fusion | flops 1600000 | bytes 320000 | tf_op jit(solution)/shard_map/convert_element_type | solution.py:16
  17.1 3.2 %fusion.51 = bf16[400,400]{1,0:T(8,128)(2,1)S(1)} fusion(), kind=kLoop, calls=%fused_computation.84 | loop fusion | flops 2080000 | bytes 320000 | tf_op jit(solution)/shard_map/neg | solution.py:20
  29.9 7.3 %all-to-all-start = ((s32[8,2,6]{2,1,0:T(2,128)}), s32[8,2,6]{2,1,0:T(2,128)S(1)}, u32[]{:S(2)}, u32[]{:S(2)}) async-start(s32[8,2,6]{2,1,0:T(2,128)} %bitcast.23), calls=%async_computation | async-start | bytes 16384 | tf_op jit(solution)/shard_map/all_to_all | solution.py:144
  38.3 3.8 %fusion.53 = (bf16[1,400,400]{2,1,0:T(8,128)(2,1)}, bf16[400,400]{1,0:T(8,128)(2,1)}) fusion(f32[]{:T(128)S(6)} %mul.305, s32[400]{0:T(512)S(1)} %fusion.65), kind=kLoop, calls=%fused_computation.89 | loop fusion | flops 960000 | bytes 641604 | tf_op jit(solution)/shard_map/concatenate | solution.py:102
  42.1 3.0 %negate_convert_fusion = bf16[1,400,400]{2,1,0:T(8,128)(2,1)S(1)} fusion(f32[]{:T(128)S(6)} %mul.305, s32[400]{0:T(512)S(1)} %fusion.65), kind=kLoop, calls=%fused_computation.51 | loop fusion | flops 960000 | bytes 321604 | tf_op jit(solution)/shard_map/convert_element_type | solution.py:71
  45.5 3.1 %copy.28 = f32[400,800]{1,0:T(8,128)} copy(f32[400,800]{0,1:T(8,128)} %bitcast.75) | data formatting | bytes 2560000 | tf_op jit(solution)/shard_map/reshape | solution.py:44
  49.3 2.1 scatter_fusion.1
  51.4 6.0 %all-to-all-start.3 = ((bf16[16,16,400]{2,1,0:T(8,128)(2,1)}), bf16[16,16,400]{2,1,0:T(8,128)(2,1)}, u32[]{:S(2)}, u32[]{:S(2)}) async-start(bf16[16,16,400]{2,1,0:T(8,128)(2,1)} %scatter_fusion.1), calls=%async_computation.3 | async-start | bytes 524288 | tf_op jit(solution)/shard_map/all_to_all | solution.py:143
  57.8 2.7 %gather_fusion = bf16[256,800]{1,0:T(8,128)(2,1)S(1)} fusion(bf16[2,128,800]{2,1,0:T(8,128)(2,1)S(1)} %copy.30, s32[256]{0:T(256)S(1)} %reshape.583), kind=kCustom, calls=%fused_computation | custom fusion | bytes 821248 | tf_op jit(solution)/shard_map/gather | solution.py:150
  63.7 94.8 %all-reduce.2.cloned.1.call-done = f32[400,400]{1,0:T(8,128)} async-done(((f32[400,400]{1,0:T(8,128)}), f32[400,400]{1,0:T(8,128)}) %all-reduce.2.cloned.1.call-update) | async-done | bytes 640016 | tf_op jit(solution)/shard_map/psum | solution.py:97
  158.5 2.4 fusion.73
  162.3 2.2 scatter_fusion
  164.4 5.8 %all-to-all-start.2 = ((bf16[16,16,800]{2,1,0:T(8,128)(2,1)}), bf16[16,16,800]{2,1,0:T(8,128)(2,1)}, u32[]{:S(2)}, u32[]{:S(2)}) async-start(bf16[16,16,800]{2,1,0:T(8,128)(2,1)} %scatter_fusion), calls=%async_computation.2 | async-start | bytes 917504 | tf_op jit(solution)/shard_map/all_to_all | solution.py:142
  174.5 2.0 fusion.48
  176.5 5.8 %all-to-all-done.2 = bf16[16,16,800]{2,1,0:T(8,128)(2,1)} async-done(((bf16[16,16,800]{2,1,0:T(8,128)(2,1)}), bf16[16,16,800]{2,1,0:T(8,128)(2,1)}, u32[]{:S(2)}, u32[]{:S(2)}) %all-to-all-start.2) | async-done | bytes 409632 | tf_op jit(solution)/shard_map/all_to_all | solution.py:142
  182.4 2.3 reshape.579
  188.1 2.6 %multiply_add_fusion = (f32[16,16,800]{2,1,0:T(8,128)}, bf16[16,16,800]{2,1,0:T(8,128)(2,1)}) fusion(f32[16,16,800]{2,1,0:T(8,128)} %reshape.580, f32[16]{0:T(128)S(1)} %get-tuple-element.8, f32[16]{0:T(128)S(1)} %broadcast_subtract_fusion, bf16[16,16,800]{2,1,0:T(8,128)(2,1)} %all-to-all-done.2, f32[16]{0:T(128)S(1)} %get-tuple-element.9, ...), kind=kLoop, calls=%fused_computation.38 | loop fusion | flops 1843200 | bytes 4096192 | tf_op jit(solution)/shard_map/add | solution.py:157
  190.7 3.8 %all-to-all-start.1 = ((bf16[16,16,800]{2,1,0:T(8,128)(2,1)}), bf16[16,16,800]{2,1,0:T(8,128)(2,1)S(1)}, u32[]{:S(2)}, u32[]{:S(2)}) async-start(bf16[16,16,800]{2,1,0:T(8,128)(2,1)} %get-tuple-element.27), calls=%async_computation.1 | async-start | bytes 917504 | tf_op jit(solution)/shard_map/all_to_all | solution.py:155
  196.0 17.0 %scatter_fusion.2 = f32[2,128,1200]{2,1,0:T(8,128)S(1)} fusion(f32[2,128,1200]{2,1,0:T(8,128)S(1)} %broadcast_in_dim.29, s32[256]{0:T(256)S(1)} %reshape.621, f32[256,1200]{1,0:T(8,128)S(1)} %bitcast.77), kind=kCustom, calls=%fused_computation.5 | custom fusion | flops 307200 | bytes 3688448 | tf_op jit(solution)/shard_map/scatter-add | solution.py:162
  214.0 3.9 %sine_convert_fusion.1 = bf16[400,400]{1,0:T(8,128)(2,1)} fusion(), kind=kLoop, calls=%fused_computation.59 | loop fusion | flops 1600000 | bytes 320000 | tf_op jit(solution)/shard_map/convert_element_type | solution.py:16
  218.5 3.8 %fusion.16 = bf16[400,800]{1,0:T(8,128)(2,1)} fusion(bf16[400,400]{1,0:T(8,128)(2,1)} %copy-done.13, bf16[400,400]{1,0:T(8,128)(2,1)} %copy-done.14, bf16[400,400]{1,0:T(8,128)(2,1)} %sine_convert_fusion.1, f32[400,800]{1,0:T(8,128)S(1)} %copy-done.10, f32[400,400]{1,0:T(8,128)S(1)} %copy-done.11, bf16[400,400]{1,0:T(8,128)(2,1)} %get-tuple-element.23, ...), kind=kOutput, calls=%fused_computation.24 | convolution fusion | flops 522240000 | bytes 4045600 | tf_op jit(solution)/shard_map/nyj,jk->nyk/dot_general | solution.py:49
  225.4 12.5 %reduce-scatter.2.cloned.1.call-done = bf16[2,32,1200]{2,1,0:T(8,128)(2,1)} async-done(((bf16[2,128,1200]{2,1,0:T(8,128)(2,1)}), bf16[2,32,1200]{2,1,0:T(8,128)(2,1)}) %reduce-scatter.2.cloned.1.call-update) | async-done | bytes 153616 | tf_op jit(solution)/shard_map/reduce_scatter | solution.py:165
  (108 shorter events, 31.9 us)
Async XLA Ops:
  7.2 13.9 %copy-start = (bf16[1,400,400]{2,1,0:T(8,128)(2,1)S(1)}, bf16[1,400,400]{2,1,0:T(8,128)(2,1)}, u32[]{:S(2)}) copy-start(bf16[1,400,400]{2,1,0:T(8,128)(2,1)} %param.8) | copy-start | bytes 960004
  7.2 151.4 %all-reduce.2.cloned.1.call-start = ((), (), s32[]{:S(2)}) async-start(), calls=%async_computation.5 | async-start | bytes 1638400 | tf_op jit(solution)/shard_map/psum | solution.py:97
  10.7 12.3 %copy-start.6 = (bf16[1,400,400]{2,1,0:T(8,128)(2,1)}, bf16[1,400,400]{2,1,0:T(8,128)(2,1)S(1)}, u32[]{:S(2)}) copy-start(bf16[1,400,400]{2,1,0:T(8,128)(2,1)S(1)} %get-tuple-element.29) | copy-start | bytes 960004
  13.9 9.0 %copy-start.8 = (bf16[1,400,400]{2,1,0:T(8,128)(2,1)}, bf16[1,400,400]{2,1,0:T(8,128)(2,1)S(1)}, u32[]{:S(2)}) copy-start(bf16[1,400,400]{2,1,0:T(8,128)(2,1)S(1)} %fusion.52) | copy-start | bytes 960004
  17.1 3.2 %copy-start.13 = (bf16[400,400]{1,0:T(8,128)(2,1)}, bf16[400,400]{1,0:T(8,128)(2,1)S(1)}, u32[]{:S(2)}) copy-start(bf16[400,400]{1,0:T(8,128)(2,1)S(1)} %cosine_convert_fusion.1) | copy-start | bytes 960004
  26.3 1.9 copy-start.16
  26.3 2.3 copy-start.17
  26.3 2.3 copy-start.18
  26.3 2.3 copy-start.19
  26.3 10.8 %copy-start.20 = (f32[64]{0:T(128)S(1)}, f32[64]{0:T(128)}, u32[]{:S(2)}) copy-start(f32[64]{0:T(128)} %param.10) | copy-start | bytes 772
  27.5 17.7 %copy-start.15 = (bf16[2,128,800]{1,2,0:T(8,128)(2,1)S(1)}, bf16[2,128,800]{1,2,0:T(8,128)(2,1)}, u32[]{:S(2)}) copy-start(bf16[2,128,800]{1,2,0:T(8,128)(2,1)} %param.15) | copy-start | bytes 1228804
  29.9 21.6 %all-to-all-start = ((s32[8,2,6]{2,1,0:T(2,128)}), s32[8,2,6]{2,1,0:T(2,128)S(1)}, u32[]{:S(2)}, u32[]{:S(2)}) async-start(s32[8,2,6]{2,1,0:T(2,128)} %bitcast.23), calls=%async_computation | async-start | bytes 16384 | tf_op jit(solution)/shard_map/all_to_all | solution.py:144
  51.4 113.0 %all-to-all-start.3 = ((bf16[16,16,400]{2,1,0:T(8,128)(2,1)}), bf16[16,16,400]{2,1,0:T(8,128)(2,1)}, u32[]{:S(2)}, u32[]{:S(2)}) async-start(bf16[16,16,400]{2,1,0:T(8,128)(2,1)} %scatter_fusion.1), calls=%async_computation.3 | async-start | bytes 524288 | tf_op jit(solution)/shard_map/all_to_all | solution.py:143
  158.5 2.4 copy-start.5
  164.4 17.9 %all-to-all-start.2 = ((bf16[16,16,800]{2,1,0:T(8,128)(2,1)}), bf16[16,16,800]{2,1,0:T(8,128)(2,1)}, u32[]{:S(2)}, u32[]{:S(2)}) async-start(bf16[16,16,800]{2,1,0:T(8,128)(2,1)} %scatter_fusion), calls=%async_computation.2 | async-start | bytes 917504 | tf_op jit(solution)/shard_map/all_to_all | solution.py:142
  186.2 2.0 copy-start.2
  186.2 1.9 copy-start.3
  190.7 3.9 %copy-start.4 = (f32[16,16,800]{2,1,0:T(8,128)S(1)}, f32[16,16,800]{2,1,0:T(8,128)}, u32[]{:S(2)}) copy-start(f32[16,16,800]{2,1,0:T(8,128)} %get-tuple-element.26) | copy-start | bytes 2457604
  190.7 27.1 %all-to-all-start.1 = ((bf16[16,16,800]{2,1,0:T(8,128)(2,1)}), bf16[16,16,800]{2,1,0:T(8,128)(2,1)S(1)}, u32[]{:S(2)}, u32[]{:S(2)}) async-start(bf16[16,16,800]{2,1,0:T(8,128)(2,1)} %get-tuple-element.27), calls=%async_computation.1 | async-start | bytes 917504 | tf_op jit(solution)/shard_map/all_to_all | solution.py:155
  194.5 43.3 %reduce-scatter.2.cloned.1.call-start = ((), (), s32[]{:S(2)}) async-start(), calls=%async_computation.6 | async-start | bytes 819200 | tf_op jit(solution)/shard_map/reduce_scatter | solution.py:165
  213.0 5.5 %copy-start.11 = (f32[400,400]{1,0:T(8,128)S(1)}, f32[400,400]{1,0:T(8,128)}, u32[]{:S(2)}) copy-start(f32[400,400]{1,0:T(8,128)} %get-tuple-element.13) | copy-start | bytes 1920004
  213.9 4.5 %copy-start.10 = (f32[400,800]{1,0:T(8,128)S(1)}, f32[400,800]{1,0:T(8,128)}, u32[]{:S(2)}) copy-start(f32[400,800]{1,0:T(8,128)} %copy.28) | copy-start | bytes 3840004
  222.3 1.5 copy-start.7
  222.3 1.5 copy-start.9
  (3 other events, 3.1 us)
Sparse Core Ops, SparseCore 0:
  27.7 130.8 all-reduce.1
  214.1 23.7 reduce-scatter.1
where the time goes:
time: 248 us; the launch traced here: 247 us
  waiting for transfers between devices  113 us (46%)
  other arithmetic  58.7 us (24%)
  local copies, waits for them, and re-layouts  30.7 us (12%)
  starting transfers between devices  22.9 us (9%)
  between operations  15.8 us (6%)
  matrix products  6.11 us (2%)
    psum x1, waiting for transfers between devices, body(): power_all = lax.psum(power_sum, ('img', 'slab'))  94.8 us
    scatter-add x1, other arithmetic, body(): numerator.at[plane_index, row_index]  17 us
    reduce_scatter x1, waiting for transfers between devices, body(): lax.psum_scatter(numerator.astype(jnp.bfloat16), 'img', scatter_dimension...  12.5 us
    convert_element_type x2, other arithmetic, dft_tables(): jnp.sin(angles).astype(jnp.bfloat16)  7.32 us
    all_to_all x1, starting transfers between devices, body(): lax.all_to_all(send_info, 'slab', split_axis=0, concat_axis=0, tiled=True)  7.25 us
    neg x2, other arithmetic, forward_tables(): right_table = jnp.concatenate([cosine_table, -sine_table], axis=1)  6.42 us
    all_to_all x1, starting transfers between devices, body(): lax.all_to_all(send_contrast, 'slab', split_axis=0, concat_axis=0, tiled=...  5.99 us
    all_to_all x1, waiting for transfers between devices, body(): lax.all_to_all(send_blocks, 'slab', split_axis=0, concat_axis=0, tiled=True)  5.84 us
  transfers between devices with their start and end apart: 6, of which 3 were waited for; matrix products, arithmetic and copies ran while one was open for 26% of the time, Pallas kernels for 0%

commit v1 on v0

--- a/solution.py
+++ b/solution.py
@@ -7,6 +7,9 @@
 RB = 16
 LOW = 4
 WL = 8
+name_ranges_by_axis = lambda point, shard_axis: jnp.sum(
+    lax.all_gather(point, axis_name=shard_axis), axis=0
+)
 
 
 def dft_tables(box_size):
@@ -94,7 +97,7 @@
     real_part = spectrum[..., :box_size]
     imag_part = spectrum[..., box_size:]
     power_sum = jnp.sum(real_part * real_part + imag_part * imag_part, axis=0)
-    power_all = lax.psum(power_sum, ("img", "slab"))
+    power_all = name_ranges_by_axis(power_sum, ("img", "slab"))
     noise_level = jnp.sqrt(power_all / (particles * device_count) + 1e-06)
     whitened = spectrum / jnp.concatenate([noise_level, noise_level], axis=1)
     row_all = jnp.arange(box_size, dtype=jnp.int32)[None, :]

time: 248 us -> 314 us (1.27)
  waiting for transfers between devices: 113 us -> 150 us
  other arithmetic: 58.7 us -> 79.3 us
  local copies, waits for them, and re-layouts: 30.7 us -> 42 us
    all_gather x0 -> x1, waiting for transfers between devices: none -> 131 us  [lax.all_gather(point, axis_name=shard_axis)]
    psum x1 -> x0, waiting for transfers between devices: 94.8 us -> none  [body(): power_all = lax.psum(power_sum, ('img', 'slab'))]
    scatter-add x1, other arithmetic: 17 us -> 27.9 us  [body(): numerator.at[plane_index, row_index]]
    reduce_sum x1, other arithmetic: 1.19 us -> 10.6 us  [jnp.sum(lax.all_gather(point, axis_name=shard_axis), axis=0)]
    unnamed x44 -> x57, local copies, waits for them, and re-layouts: 3.65 us -> 7.76 us
    reshape x2 -> x0, local copies, waits for them, and re-layouts: 3.56 us -> none  [transform(): return spectrum.reshape(batch_size, box_size, 2 * box_size)]
  transfers between devices with their start and end apart: 6 -> 6, of which waited for: 3 -> 3; matrix products, arithmetic and copies ran while one was open for 26% -> 29% of each run, Pallas kernels for 0% -> 0%
where the time goes in v1:
time: 314 us; the launch traced here: 313 us
  waiting for transfers between devices  150 us (48%)
  other arithmetic  79.3 us (25%)
  local copies, waits for them, and re-layouts  42 us (13%)
  starting transfers between devices  21.9 us (7%)
  between operations  15.8 us (5%)
  matrix products  3.38 us (1%)
    all_gather x1, waiting for transfers between devices, lax.all_gather(point, axis_name=shard_axis)  131 us
    scatter-add x1, other arithmetic, body(): numerator.at[plane_index, row_index]  27.9 us
    reduce_scatter x1, waiting for transfers between devices, body(): lax.psum_scatter(numerator.astype(jnp.bfloat16), 'img', scatter_dimension...  12.4 us
    reduce_sum x1, other arithmetic, jnp.sum(lax.all_gather(point, axis_name=shard_axis), axis=0)  10.6 us
    unnamed x57, local copies, waits for them, and re-layouts  7.76 us
    convert_element_type x2, other arithmetic, dft_tables(): jnp.sin(angles).astype(jnp.bfloat16)  7.56 us
    all_to_all x1, starting transfers between devices, body(): lax.all_to_all(send_info, 'slab', split_axis=0, concat_axis=0, tiled=True)  7.25 us
    all_to_all x1, waiting for transfers between devices, body(): lax.all_to_all(send_blocks, 'slab', split_axis=0, concat_axis=0, tiled=True)  6.53 us
  transfers between devices with their start and end apart: 6, of which 3 were waited for; matrix products, arithmetic and copies ran while one was open for 29% of the time, Pallas kernels for 0%

profile of v1, /device:TPU:0, one launch (start us, length us, event | category | flops | bytes accessed | tf_op | source)
XLA Modules:
  0.0 312.5 jit_solution(1700866827599551254)
XLA Ops:
  7.2 3.5 %sine_convert_fusion = (bf16[1,400,400]{2,1,0:T(8,128)(2,1)S(1)}, bf16[1,400,400]{2,1,0:T(8,128)(2,1)S(1)}) fusion(), kind=kLoop, calls=%fused_computation.53 | loop fusion | flops 1760000 | bytes 640000 | tf_op jit(solution)/shard_map/convert_element_type | solution.py:19
  10.7 3.2 %fusion.42 = bf16[1,400,400]{2,1,0:T(8,128)(2,1)S(1)} fusion(), kind=kLoop, calls=%fused_computation.76 | loop fusion | flops 2080000 | bytes 320000 | tf_op jit(solution)/shard_map/neg | solution.py:23
  13.9 4.1 %sine_convert_fusion.1 = (bf16[400,400]{1,0:T(8,128)(2,1)}, bf16[400,400]{1,0:T(8,128)(2,1)S(1)}) fusion(), kind=kLoop, calls=%fused_computation.58 | loop fusion | flops 1760000 | bytes 640000 | tf_op jit(solution)/shard_map/convert_element_type | solution.py:19
  18.0 3.2 %fusion.41 = bf16[400,400]{1,0:T(8,128)(2,1)S(1)} fusion(), kind=kLoop, calls=%fused_computation.75 | loop fusion | flops 2080000 | bytes 320000 | tf_op jit(solution)/shard_map/neg | solution.py:23
  29.9 7.3 %all-to-all-start = ((s32[8,2,6]{2,1,0:T(2,128)}), s32[8,2,6]{2,1,0:T(2,128)S(1)}, u32[]{:S(2)}, u32[]{:S(2)}) async-start(s32[8,2,6]{2,1,0:T(2,128)} %bitcast.22), calls=%async_computation | async-start | bytes 16384 | tf_op jit(solution)/shard_map/all_to_all | solution.py:147
  38.4 3.0 negate_convert_fusion
  41.4 3.8 %fusion.43 = (bf16[1,400,400]{1,2,0:T(8,128)(2,1)}, bf16[400,400]{0,1:T(8,128)(2,1)}) fusion(f32[]{:T(128)S(6)} %mul.305, s32[400]{0:T(512)S(1)} %fusion.55), kind=kLoop, calls=%fused_computation.78 | loop fusion | flops 960000 | bytes 641604 | tf_op jit(solution)/shard_map/concatenate | solution.py:105
  48.3 6.0 %all-to-all-start.3 = ((bf16[16,16,400]{2,1,0:T(8,128)(2,1)}), bf16[16,16,400]{2,1,0:T(8,128)(2,1)}, u32[]{:S(2)}, u32[]{:S(2)}) async-start(bf16[16,16,400]{2,1,0:T(8,128)(2,1)} %scatter_fusion.1), calls=%async_computation.3 | async-start | bytes 524288 | tf_op jit(solution)/shard_map/all_to_all | solution.py:146
  54.7 3.4 %gather_fusion = bf16[256,800]{1,0:T(8,128)(2,1)} fusion(bf16[2,128,800]{2,1,0:T(8,128)(2,1)S(1)} %copy.37, s32[256]{0:T(256)S(1)} %reshape.575), kind=kCustom, calls=%fused_computation | custom fusion | bytes 821248 | tf_op jit(solution)/shard_map/gather | solution.py:153
  58.1 2.3 reshape.574
  63.6 131.1 %all-gather.2.cloned.1.call-done = f32[32,400,400]{2,1,0:T(8,128)} async-done(((f32[1,400,400]{2,1,0:T(8,128)}), f32[32,400,400]{2,1,0:T(8,128)}) %all-gather.2.cloned.1.call-update) | async-done | bytes 20480016 | tf_op jit(solution)/shard_map/all_gather | solution.py:11
  194.8 10.6 %reduce_sum.33 = f32[400,400]{1,0:T(8,128)} reduce(f32[32,400,400]{2,1,0:T(8,128)} %all-gather.2.cloned.1.call-done, f32[]{:T(128)} %constant.22.clone.1), dimensions={0}, to_apply=%region_0.1 | reduce | flops 4960000 | bytes 21120004 | tf_op jit(solution)/shard_map/reduce_sum | solution.py:10
  211.9 2.4 scatter_fusion
  214.3 4.3 %all-to-all-start.2 = ((bf16[16,16,800]{2,1,0:T(8,128)(2,1)}), bf16[16,16,800]{2,1,0:T(8,128)(2,1)}, u32[]{:S(2)}, u32[]{:S(2)}) async-start(bf16[16,16,800]{2,1,0:T(8,128)(2,1)} %scatter_fusion), calls=%async_computation.2 | async-start | bytes 917504 | tf_op jit(solution)/shard_map/all_to_all | solution.py:145
  220.4 3.2 %reshape.567 = f32[16,16,800]{2,1,0:T(8,128)} reshape(f32[16,16,2,400]{3,2,1,0:T(2,128)} %pad_maximum_fusion) | data formatting | bytes 1638400 | tf_op jit(solution)/shard_map/reshape | solution.py:84
  225.7 6.5 %all-to-all-done.2 = bf16[16,16,800]{2,1,0:T(8,128)(2,1)} async-done(((bf16[16,16,800]{2,1,0:T(8,128)(2,1)}), bf16[16,16,800]{2,1,0:T(8,128)(2,1)}, u32[]{:S(2)}, u32[]{:S(2)}) %all-to-all-start.2) | async-done | bytes 409632 | tf_op jit(solution)/shard_map/all_to_all | solution.py:145
  232.2 2.3 reshape.571
  234.9 2.1 pad_maximum_fusion.1
  237.0 3.2 %reshape.572 = f32[16,16,800]{2,1,0:T(8,128)} reshape(f32[16,16,2,400]{3,2,1,0:T(2,128)} %pad_maximum_fusion.1) | data formatting | bytes 1638400 | tf_op jit(solution)/shard_map/reshape | solution.py:84
  240.3 2.9 multiply_add_fusion
  243.2 4.2 %all-to-all-start.1 = ((bf16[16,16,800]{2,1,0:T(8,128)(2,1)}), bf16[16,16,800]{2,1,0:T(8,128)(2,1)}, u32[]{:S(2)}, u32[]{:S(2)}) async-start(bf16[16,16,800]{2,1,0:T(8,128)(2,1)} %get-tuple-element.29), calls=%async_computation.1 | async-start | bytes 917504 | tf_op jit(solution)/shard_map/all_to_all | solution.py:158
  250.3 27.9 %scatter_fusion.2 = f32[2,128,1200]{2,1,0:T(8,128)S(1)} fusion(f32[2,128,1200]{2,1,0:T(8,128)S(1)} %broadcast_in_dim.29, s32[256]{0:T(256)S(1)} %reshape.613, f32[256,1200]{1,0:T(8,128)} %bitcast.75), kind=kCustom, calls=%fused_computation.5 | custom fusion | flops 307200 | bytes 3688448 | tf_op jit(solution)/shard_map/scatter-add | solution.py:165
  279.2 2.4 gather_fusion.1
  290.6 12.4 %reduce-scatter.2.cloned.1.call-done = bf16[2,32,1200]{2,1,0:T(8,128)(2,1)} async-done(((bf16[2,128,1200]{2,1,0:T(8,128)(2,1)}), bf16[2,32,1200]{2,1,0:T(8,128)(2,1)}) %reduce-scatter.2.cloned.1.call-update) | async-done | bytes 153616 | tf_op jit(solution)/shard_map/reduce_scatter | solution.py:168
  (123 shorter events, 41.2 us)
Async XLA Ops:
  7.2 14.8 %copy-start = (bf16[1,400,400]{2,1,0:T(8,128)(2,1)S(1)}, bf16[1,400,400]{2,1,0:T(8,128)(2,1)}, u32[]{:S(2)}) copy-start(bf16[1,400,400]{2,1,0:T(8,128)(2,1)} %param.8) | copy-start | bytes 960004
  7.2 187.6 %all-gather.2.cloned.1.call-start = ((), (), s32[]{:S(2)}) async-start(), calls=%async_computation.5 | async-start | bytes 27033600 | tf_op jit(solution)/shard_map/all_gather | solution.py:11
  10.7 13.2 %copy-start.10 = (bf16[1,400,400]{2,1,0:T(8,128)(2,1)}, bf16[1,400,400]{2,1,0:T(8,128)(2,1)S(1)}, u32[]{:S(2)}) copy-start(bf16[1,400,400]{2,1,0:T(8,128)(2,1)S(1)} %get-tuple-element.31) | copy-start | bytes 960004
  13.9 10.0 %copy-start.12 = (bf16[1,400,400]{2,1,0:T(8,128)(2,1)}, bf16[1,400,400]{2,1,0:T(8,128)(2,1)S(1)}, u32[]{:S(2)}) copy-start(bf16[1,400,400]{2,1,0:T(8,128)(2,1)S(1)} %fusion.42) | copy-start | bytes 960004
  18.0 3.2 %copy-start.16 = (bf16[400,400]{1,0:T(8,128)(2,1)}, bf16[400,400]{1,0:T(8,128)(2,1)S(1)}, u32[]{:S(2)}) copy-start(bf16[400,400]{1,0:T(8,128)(2,1)S(1)} %get-tuple-element.33) | copy-start | bytes 960004
  26.2 2.1 copy-start.22
  26.2 2.1 copy-start.23
  26.2 2.1 copy-start.24
  26.3 2.2 copy-start.21
  26.3 10.9 %copy-start.25 = (f32[64]{0:T(128)S(1)}, f32[64]{0:T(128)}, u32[]{:S(2)}) copy-start(f32[64]{0:T(128)} %param.10) | copy-start | bytes 772
  27.5 17.7 %copy-start.20 = (bf16[2,128,800]{1,2,0:T(8,128)(2,1)S(1)}, bf16[2,128,800]{1,2,0:T(8,128)(2,1)}, u32[]{:S(2)}) copy-start(bf16[2,128,800]{1,2,0:T(8,128)(2,1)} %param.15) | copy-start | bytes 1228804
  29.9 18.4 %all-to-all-start = ((s32[8,2,6]{2,1,0:T(2,128)}), s32[8,2,6]{2,1,0:T(2,128)S(1)}, u32[]{:S(2)}, u32[]{:S(2)}) async-start(s32[8,2,6]{2,1,0:T(2,128)} %bitcast.22), calls=%async_computation | async-start | bytes 16384 | tf_op jit(solution)/shard_map/all_to_all | solution.py:147
  48.3 166.0 %all-to-all-start.3 = ((bf16[16,16,400]{2,1,0:T(8,128)(2,1)}), bf16[16,16,400]{2,1,0:T(8,128)(2,1)}, u32[]{:S(2)}, u32[]{:S(2)}) async-start(bf16[16,16,400]{2,1,0:T(8,128)(2,1)} %scatter_fusion.1), calls=%async_computation.3 | async-start | bytes 524288 | tf_op jit(solution)/shard_map/all_to_all | solution.py:146
  60.5 3.2 %copy-start.1 = (f32[16,16,2,400]{3,2,1,0:T(2,128)}, f32[16,16,2,400]{3,2,1,0:T(2,128)S(1)}, u32[]{:S(2)}) copy-start(f32[16,16,2,400]{3,2,1,0:T(2,128)S(1)} %reshape.574) | copy-start | bytes 2457604
  60.5 2.1 copy-start.3
  208.5 10.2 %slice-start = ((f32[16,16,2,400]{3,2,1,0:T(2,128)}), f32[16,16,2,1]{3,2,1,0:T(2,128)S(1)}, s32[]{:S(2)}) async-start(f32[16,16,2,400]{3,2,1,0:T(2,128)} %copy-done.1), calls=%async_computation.7 | async-start | bytes 524288 | tf_op jit(solution)/shard_map/jit(_roll_static)/slice | solution.py:84
  208.5 10.2 %copy-start.2 = (f32[16,16,2,399]{3,2,1,0:T(2,128)S(1)}, f32[16,16,2,399]{3,2,1,0:T(2,128)}, u32[]{:S(2)}) copy-start(f32[16,16,2,399]{3,2,1,0:T(2,128)} %slice.97) | copy-start | bytes 2451460
  214.3 17.9 %all-to-all-start.2 = ((bf16[16,16,800]{2,1,0:T(8,128)(2,1)}), bf16[16,16,800]{2,1,0:T(8,128)(2,1)}, u32[]{:S(2)}, u32[]{:S(2)}) async-start(bf16[16,16,800]{2,1,0:T(8,128)(2,1)} %scatter_fusion), calls=%async_computation.2 | async-start | bytes 917504 | tf_op jit(solution)/shard_map/all_to_all | solution.py:145
  237.0 3.2 %copy-start.4 = (f32[256,800]{1,0:T(8,128)S(1)}, f32[256,800]{1,0:T(8,128)}, u32[]{:S(2)}) copy-start(f32[256,800]{1,0:T(8,128)} %convert_element_type.272) | copy-start | bytes 2457604
  243.2 5.7 %copy-start.5 = (f32[16,16,800]{2,1,0:T(8,128)S(1)}, f32[16,16,800]{2,1,0:T(8,128)}, u32[]{:S(2)}) copy-start(f32[16,16,800]{2,1,0:T(8,128)} %get-tuple-element.28) | copy-start | bytes 2457604
  243.2 36.0 %all-to-all-start.1 = ((bf16[16,16,800]{2,1,0:T(8,128)(2,1)}), bf16[16,16,800]{2,1,0:T(8,128)(2,1)}, u32[]{:S(2)}, u32[]{:S(2)}) async-start(bf16[16,16,800]{2,1,0:T(8,128)(2,1)} %get-tuple-element.29), calls=%async_computation.1 | async-start | bytes 917504 | tf_op jit(solution)/shard_map/all_to_all | solution.py:158
  247.4 55.5 %reduce-scatter.2.cloned.1.call-start = ((), (), s32[]{:S(2)}) async-start(), calls=%async_computation.6 | async-start | bytes 819200 | tf_op jit(solution)/shard_map/reduce_scatter | solution.py:168
  279.1 6.6 %copy-start.6 = (f32[400,400]{0,1:T(8,128)S(1)}, f32[400,400]{0,1:T(8,128)}, u32[]{:S(2)}) copy-start(f32[400,400]{0,1:T(8,128)} %get-tuple-element.17) | copy-start | bytes 1920004
  279.1 6.6 %copy-start.8 = (bf16[400,400]{0,1:T(8,128)(2,1)S(1)}, bf16[400,400]{0,1:T(8,128)(2,1)}, u32[]{:S(2)}) copy-start(bf16[400,400]{0,1:T(8,128)(2,1)} %get-tuple-element.25) | copy-start | bytes 960004
  (9 other events, 12.3 us)
Sparse Core Ops, SparseCore 0:
  27.7 167.0 all-gather.1
  279.3 23.6 reduce-scatter.1
